TPU v7x, 512 devices: a whole 4x8x8 slice. The times are simulated.
512 devices in a mesh: space: 64 (over x, y, core), chan: 8 (over z).
Axes of the slice: x: 4, y: 8, z: 8, core: 2. Of those that a mesh axis runs over, the one named last changes fastest.
Arguments:
- features: bfloat16 [128, 64, 4096], P('space', 'chan'), may hold values from -6 to 6
- conv_weight: bfloat16 [128, 9, 64], P('chan'), may hold values from -0.25 to 0.25
- down_weight: bfloat16 [128, 4, 128], P('chan'), may hold values from -0.25 to 0.25
- cotangent: bfloat16 [128, 128, 1024], P('space', 'chan'), may hold values from -16 to 16
- partner: int32 [128, 4], P('space'), may hold values from 0 to 511, as said below
- orientation: int32 [128, 4], P('space'), may hold values from 0 to 1, as said below
Outputs:
- pooled: bfloat16 [128, 128, 1024], P('space', 'chan')
- features_grad: bfloat16 [128, 64, 4096], P('space', 'chan')
- conv_grad: float32 [128, 9, 64], P('chan')
- down_grad: float32 [128, 4, 128], P('chan')
Inputs may be any that keep to these rules, and one draw needn't show every extreme that they name: Bordering is mutual: the slot at partner[t, e] has partner 4 t + e; no edge borders itself; every slot 0 to 511 appears exactly once. `orientation`: both edges of a bordering pair carry the same value.
All inputs are finite; a program needn't handle non-finite values.
Results may differ from a plain program's by a relative error of at most 0.0049.
Values may be sent and summed in bfloat16 or wider, within the bound.
No kernel may reach another device: no remote copies, remote signals or barrier semaphores. Data moves between devices by JAX's collectives and lax.ppermute only.
A program may use at most 64 MiB of HBM per device.

v0:
```python
import jax
import jax.numpy as jnp
from jax import lax
from jax.sharding import PartitionSpec as P

S = 64


def edge_strips(values):
    return jnp.stack(
        [values[..., 0, :], values[..., :, -1], values[..., -1, :], values[..., :, 0]], axis=-3
    )


def rim_strips(padded):
    return jnp.stack(
        [padded[..., 0, 1:-1], padded[..., 1:-1, -1], padded[..., -1, 1:-1], padded[..., 1:-1, 0]],
        axis=-3,
    )


def bordering(strips, partner, orientation):
    flat = strips.reshape((-1,) + strips.shape[2:])
    picked = jnp.take(flat, partner.reshape(-1), axis=0)
    picked = picked.reshape(partner.shape + strips.shape[2:])
    return jnp.where((orientation == 1)[..., None, None], picked[..., ::-1], picked)


def pad_tile(values, halo_strips):
    tile_side = values.shape[-1]
    widths = [(0, 0)] * (values.ndim - 2) + [(1, 1), (1, 1)]
    padded = jnp.pad(values, widths)
    padded = padded.at[..., 0, 1 : tile_side + 1].set(halo_strips[..., 0, :, :])
    padded = padded.at[..., 1 : tile_side + 1, tile_side + 1].set(halo_strips[..., 1, :, :])
    padded = padded.at[..., tile_side + 1, 1 : tile_side + 1].set(halo_strips[..., 2, :, :])
    return padded.at[..., 1 : tile_side + 1, 0].set(halo_strips[..., 3, :, :])


def add_edges(interior, returned):
    interior = interior.at[..., 0, :].add(returned[..., 0, :, :])
    interior = interior.at[..., :, -1].add(returned[..., 1, :, :])
    interior = interior.at[..., -1, :].add(returned[..., 2, :, :])
    return interior.at[..., :, 0].add(returned[..., 3, :, :])


def unfold(padded, height, width):
    taps = [
        padded[..., row_shift : row_shift + height, col_shift : col_shift + width]
        for row_shift in range(3)
        for col_shift in range(3)
    ]
    return jnp.stack(taps, axis=-4)


def fold_taps(taps):
    total = None
    for row_shift in range(3):
        for col_shift in range(3):
            piece = taps[..., 3 * row_shift + col_shift, :, :, :]
            widths = [(0, 0)] * (piece.ndim - 2) + [
                (row_shift, 2 - row_shift),
                (col_shift, 2 - col_shift),
            ]
            placed = jnp.pad(piece, widths)
            total = placed if total is None else total + placed
    return total


def silu_grad(values):
    gate = jax.nn.sigmoid(values)
    return gate * (1.0 + values * (1.0 - gate))


def shards(features, conv_weight, down_weight, cotangent, partner, orientation):
    tile_count = features.shape[0]
    tile_side = S
    chan_count = lax.axis_size("chan")
    chan_index = lax.axis_index("chan")
    chan_part = features.shape[1]
    block_rows = tile_side // chan_count
    whole_features = lax.all_gather(features, "chan", axis=1, tiled=True)
    in_channels = whole_features.shape[1]
    images = whole_features.reshape(tile_count, in_channels, tile_side, tile_side)
    gathered = lax.all_gather(edge_strips(images), "space", axis=0, tiled=True)
    halo_strips = bordering(gathered, partner, orientation)
    padded = pad_tile(images, halo_strips)
    block = lax.dynamic_slice_in_dim(padded, chan_index * block_rows, block_rows + 2, 2)
    conv_full, down_full = (
        lax.all_gather(conv_weight, "chan", axis=0, tiled=True),
        lax.all_gather(down_weight, "chan", axis=0, tiled=True),
    )
    out_channels = conv_full.shape[0]
    columns = unfold(block, block_rows, tile_side)
    pre_act = jnp.einsum("okc,tkcrs->tors", conv_full, columns, preferred_element_type=jnp.float32)
    activated = jax.nn.silu(pre_act).astype(jnp.bfloat16)
    quads = activated.reshape(tile_count, out_channels, block_rows // 2, 2, tile_side // 2, 2)
    down_taps = down_full.reshape(out_channels, 2, 2, out_channels)
    pooled_rows = jnp.einsum(
        "opqc,tcipjq->toij", down_taps, quads, preferred_element_type=jnp.float32
    ).astype(jnp.bfloat16)
    pooled_band = pooled_rows.reshape(tile_count, out_channels, block_rows // 2 * (tile_side // 2))
    pooled = lax.all_to_all(pooled_band, "chan", split_axis=1, concat_axis=2, tiled=True)
    grad_flat = lax.all_to_all(cotangent, "chan", split_axis=2, concat_axis=1, tiled=True)
    grad_band = grad_flat.reshape(tile_count, out_channels, block_rows // 2, tile_side // 2)
    down_part = jnp.einsum(
        "toij,tcipjq->opqc", grad_band, quads, preferred_element_type=jnp.float32
    )
    down_part = down_part.reshape(out_channels, 4, out_channels)
    grad_act = jnp.einsum(
        "opqc,toij->tcipjq", down_taps, grad_band, preferred_element_type=jnp.float32
    )
    grad_act = grad_act.reshape(tile_count, out_channels, block_rows, tile_side)
    grad_pre = (grad_act * silu_grad(pre_act)).astype(jnp.bfloat16)
    conv_part = jnp.einsum("tors,tkcrs->okc", grad_pre, columns, preferred_element_type=jnp.float32)
    grad_block = fold_taps(
        jnp.einsum("okc,tors->tkcrs", conv_full, grad_pre, preferred_element_type=jnp.float32)
    )
    row_blocks = lax.all_to_all(
        grad_block[None].astype(jnp.bfloat16), "chan", split_axis=2, concat_axis=0, tiled=True
    ).astype(jnp.float32)
    stacked = jnp.moveaxis(row_blocks, 0, 2)
    inner = stacked[:, :, :, 1 : block_rows + 1, :].reshape(
        tile_count, chan_part, tile_side, tile_side + 2
    )
    grad_padded = jnp.pad(inner, ((0, 0), (0, 0), (1, 1), (0, 0)))
    grad_padded = grad_padded.at[:, :, 0:tile_side:block_rows, :].add(stacked[:, :, :, 0, :])
    grad_padded = grad_padded.at[:, :, block_rows + 1 : tile_side + 2 : block_rows, :].add(
        stacked[:, :, :, block_rows + 1, :]
    )
    rim_all = lax.all_gather(rim_strips(grad_padded), "space", axis=0, tiled=True)
    returned = bordering(rim_all, partner, orientation)
    features_grad = add_edges(grad_padded[:, :, 1:-1, 1:-1], returned).astype(jnp.bfloat16)
    features_grad = features_grad.reshape(tile_count, chan_part, tile_side * tile_side)
    grad_scale = float(lax.axis_size("space") * tile_count * tile_side * tile_side) ** (-0.5)
    share = out_channels // chan_count
    conv_total, down_total = lax.psum((conv_part, down_part), ("space", "chan"))
    conv_grad = lax.dynamic_slice_in_dim(conv_total, chan_index * share, share, 0)
    down_grad = lax.dynamic_slice_in_dim(down_total, chan_index * share, share, 0)
    return (pooled, features_grad, conv_grad * grad_scale, down_grad * grad_scale)


def solution(mesh):
    placed = (
        P("space", "chan", None),
        P("chan", None, None),
        P("chan", None, None),
        P("space", "chan", None),
        P("space", None),
        P("space", None),
    )
    return jax.shard_map(
        shards,
        mesh=mesh,
        in_specs=placed,
        out_specs=(
            P("space", "chan", None),
            P("space", "chan", None),
            P("chan", None, None),
            P("chan", None, None),
        ),
        check_vma=False,
    )
```

profile of v0, /device:TPU:1, one launch (start us, length us, event | category | flops | bytes accessed | tf_op | source)
XLA Modules:
  0.0 560.8 jit_solution(13366105239182730253)
XLA Ops:
  7.2 0.7 all-gather.4.cloned.1.call-update
  8.0 44.8 %all-gather.4.cloned.1.call-done = bf16[2,64,4096]{2,1,0:T(8,128)(2,1)} async-done(((bf16[2,8,4096]{2,1,0:T(8,128)(2,1)}), bf16[2,64,4096]{2,1,0:T(8,128)(2,1)}) %all-gather.4.cloned.1.call-update) | async-done | bytes 1048592 | tf_op jit(solution)/shard_map/all_gather | solution.py:81
  52.8 2.0 copy.217
  55.0 1.0 pad_maximum_fusion
  56.0 0.4 copy.243
  56.4 1.2 reshape.474
  57.6 4.4 all-to-all-start.1
  62.1 20.6 %all_gather.17 = bf16[128,9,64]{2,0,1:T(8,128)(2,1)S(1)} all-gather(bf16[16,9,64]{2,0,1:T(8,128)(2,1)S(1)} %copy-done.7), channel_id=1, replica_groups=mesh['space'=64,'chan'=8] {'chan'}, dimensions={0}, use_global_device_ids=true | all-gather | bytes 165888 | tf_op jit(solution)/shard_map/all_gather | solution.py:89
  82.8 18.9 %all_gather.18 = bf16[128,4,128]{2,1,0:T(4,128)(2,1)S(1)} all-gather(bf16[16,4,128]{2,1,0:T(4,128)(2,1)S(1)} %copy-done.8), channel_id=1, replica_groups=mesh['space'=64,'chan'=8] {'chan'}, dimensions={0}, use_global_device_ids=true | all-gather | bytes 147456 | tf_op jit(solution)/shard_map/all_gather | solution.py:90
  101.9 0.6 fusion.29
  102.5 0.4 reshape.475
  102.9 0.3 copy.244
  103.2 0.2 reshape.421
  103.4 0.2 convolution_bitcast_fusion.2
  103.6 1.2 copy.246
  104.8 2.6 pad.68
  107.4 40.1 %all-gather.6.cloned.1.call-done = bf16[128,4,64,64]{2,3,0,1:T(8,128)(2,1)} async-done(((bf16[2,4,64,64]{2,3,0,1:T(8,128)(2,1)}), bf16[128,4,64,64]{2,3,0,1:T(8,128)(2,1)}) %all-gather.6.cloned.1.call-update) | async-done | bytes 4194320 | tf_op jit(solution)/shard_map/all_gather | solution.py:84
  147.5 11.9 %copy.224 = bf16[128,4,64,64]{3,2,1,0:T(8,128)(2,1)} copy(bf16[128,4,64,64]{2,3,0,1:T(8,128)(2,1)} %all-gather.6.cloned.1.call-done) | data formatting | bytes 8388608 | tf_op jit(solution)/shard_map/all_gather | solution.py:84
  159.4 4.0 gather_fusion
  163.4 0.1 copy.225
  163.9 1.5 scatter.14
  165.4 1.4 scatter.15
  166.9 0.2 scatter.16
  167.1 1.4 scatter.19
  169.1 0.1 fusion.5
  169.2 0.1 fusion.4
  169.4 0.2 copy-done.5
  169.6 1.6 multiply_convert_fusion
  171.2 0.8 convolution_bitcast_fusion
  172.0 0.7 slice_bitcast_fusion.8
  172.7 0.9 fusion.1
  173.6 1.1 copy.255
  174.7 7.1 %all-to-all-start.2 = ((bf16[1,2,64,10,66]{4,1,3,0,2:T(2,128)(2,1)}), bf16[1,2,64,10,66]{4,1,3,0,2:T(2,128)(2,1)S(1)}, u32[]{:S(2)}, u32[]{:S(2)}) async-start(bf16[1,2,64,10,66]{4,1,3,0,2:T(2,128)(2,1)} %copy.255), calls=%async_computation.2 | async-start | bytes 655360 | tf_op jit(solution)/shard_map/all_to_all | solution.py:118
  181.8 2.2 fusion.15
  184.0 1.8 copy.272
  185.8 1.4 convolution_bitcast_fusion.1
  187.2 0.2 all-gather.8.cloned.1.call-start
  187.4 8.1 %all-to-all-done.2 = bf16[1,2,64,10,66]{4,1,3,0,2:T(2,128)(2,1)S(1)} async-done(((bf16[1,2,64,10,66]{4,1,3,0,2:T(2,128)(2,1)}), bf16[1,2,64,10,66]{4,1,3,0,2:T(2,128)(2,1)S(1)}, u32[]{:S(2)}, u32[]{:S(2)}) %all-to-all-start.2) | async-done | bytes 168992 | tf_op jit(solution)/shard_map/all_to_all | solution.py:118
  195.7 0.9 scatter_fusion
  196.6 0.9 scatter_fusion.1
  197.5 0.2 fusion.28
  197.7 0.2 copy.304
  198.0 0.2 copy.263
  198.3 0.6 pad_maximum_fusion.1
  199.0 0.2 fusion
  199.2 0.8 copy.240
  199.9 3.4 all-to-all-start
  203.3 7.1 %all-to-all-done = bf16[2,128,128]{2,0,1:T(2,128)(2,1)S(1)} async-done(((bf16[2,128,128]{2,0,1:T(2,128)(2,1)}), bf16[2,128,128]{2,0,1:T(2,128)(2,1)S(1)}, u32[]{:S(2)}, u32[]{:S(2)}) %all-to-all-start) | async-done | bytes 65568 | tf_op jit(solution)/shard_map/all_to_all | solution.py:102
  210.5 0.6 copy.322
  211.1 248.5 %all-reduce.14.cloned.1.call-done = (f32[128,9,64]{2,0,1:T(8,128)}, f32[128,4,128]{2,1,0:T(4,128)}) async-done(((f32[128,9,64]{2,0,1:T(8,128)}, f32[128,4,128]{2,1,0:T(4,128)}), (f32[128,9,64]{2,0,1:T(8,128)}, f32[128,4,128]{2,1,0:T(4,128)})) %all-reduce.14.cloned.1.call-update) | async-done | bytes 557072 | tf_op jit(solution)/shard_map/psum | solution.py:136
  459.6 1.4 dynamic-slice_multiply_fusion.1
  461.0 1.5 dynamic-slice_multiply_fusion
  462.5 0.2 slice.419
  462.7 0.3 copy.302
  463.0 74.2 %all-gather.8.cloned.1.call-done = f32[128,4,8,64]{3,2,0,1:T(8,128)} async-done(((f32[2,4,8,64]{3,2,0,1:T(8,128)}), f32[128,4,8,64]{3,2,0,1:T(8,128)}) %all-gather.8.cloned.1.call-update) | async-done | bytes 1048592 | tf_op jit(solution)/shard_map/all_gather | solution.py:130
  537.2 1.9 copy.264
  539.1 0.6 gather_fusion.1
  539.9 0.3 copy.266
  540.3 1.8 scatter-add.36
  542.1 0.3 copy.267
  542.4 0.2 slice_add_fusion
  542.6 10.4 %scatter-add.38 = f32[2,8,64,64]{2,1,0,3:T(8,128)S(1)} dynamic-update-slice(f32[2,8,64,64]{2,1,0,3:T(8,128)S(1)} %fusion.23, f32[2,8,1,64]{2,1,0,3:T(8,128)S(1)} %slice_add_fusion, s32[]{:T(128)} %constant.268.clone.1, s32[]{:T(128)} %constant.268.clone.1, s32[]{:T(128)} %constant.280.clone.1, s32[]{:T(128)} %constant.268.clone.1) | dynamic-update-slice | bytes 8196 | tf_op jit(solution)/shard_map/scatter-add | solution.py:42
  553.1 0.3 copy.268
  553.4 0.9 reshape.429
  (72 shorter events, 2.2 us)
Async XLA Ops:
  7.2 48.9 %copy-start.6 = (bf16[2,16,1024]{2,1,0:T(8,128)(2,1)S(1)}, bf16[2,16,1024]{2,1,0:T(8,128)(2,1)}, u32[]{:S(2)}) copy-start(bf16[2,16,1024]{2,1,0:T(8,128)(2,1)} %param.25) | copy-start | bytes 196612
  7.2 45.7 %all-gather.4.cloned.1.call-start = ((), (), s32[]{:S(2)}) async-start(), calls=%async_computation.3 | async-start | bytes 1179648 | tf_op jit(solution)/shard_map/all_gather | solution.py:81
  7.9 54.1 %copy-start.9 = (s32[2,4]{1,0:T(2,128)S(1)}, s32[2,4]{1,0:T(2,128)}, u32[]{:S(2)}) copy-start(s32[2,4]{1,0:T(2,128)} %param.26) | copy-start | bytes 100
  7.9 54.2 %copy-start.7 = (bf16[16,9,64]{2,0,1:T(8,128)(2,1)S(1)}, bf16[16,9,64]{2,0,1:T(8,128)(2,1)}, u32[]{:S(2)}) copy-start(bf16[16,9,64]{2,0,1:T(8,128)(2,1)} %param.23) | copy-start | bytes 55300
  7.9 74.8 %copy-start.10 = (s32[2,4]{1,0:T(2,128)S(1)}, s32[2,4]{1,0:T(2,128)}, u32[]{:S(2)}) copy-start(s32[2,4]{1,0:T(2,128)} %param.27) | copy-start | bytes 100
  7.9 74.8 %copy-start.8 = (bf16[16,4,128]{2,1,0:T(4,128)(2,1)S(1)}, bf16[16,4,128]{2,1,0:T(4,128)(2,1)}, u32[]{:S(2)}) copy-start(bf16[16,4,128]{2,1,0:T(4,128)(2,1)} %param.24) | copy-start | bytes 49156
  8.0 139.6 %all-gather.6.cloned.1.call-start = ((), (), s32[]{:S(2)}) async-start(), calls=%async_computation.4 | async-start | bytes 8519680 | tf_op jit(solution)/shard_map/all_gather | solution.py:84
  54.9 48.7 %copy-start = (bf16[2,64,4096]{1,2,0:T(8,128)(2,1)}, bf16[2,64,4096]{1,2,0:T(8,128)(2,1)S(1)}, u32[]{:S(2)}) copy-start(bf16[2,64,4096]{1,2,0:T(8,128)(2,1)S(1)} %copy.217) | copy-start | bytes 3145732
  57.6 44.9 %all-to-all-start.1 = ((bf16[8,2,2048]{2,1,0:T(2,128)(2,1)}), bf16[8,2,2048]{2,1,0:T(2,128)(2,1)S(1)}, u32[]{:S(2)}, u32[]{:S(2)}) async-start(bf16[8,2,2048]{2,1,0:T(2,128)(2,1)} %reshape.474), calls=%async_computation.1 | async-start | bytes 131072 | tf_op jit(solution)/shard_map/all_to_all | solution.py:103
  101.9 5.5 copy-start.3
  168.5 1.0 copy-start.5
  169.4 1.8 copy-start.1
  173.6 12.2 %copy-start.2 = (bf16[2,9,64,8,64]{2,4,1,3,0:T(8,128)(2,1)S(1)}, bf16[2,9,64,8,64]{2,4,1,3,0:T(8,128)(2,1)}, u32[]{:S(2)}) copy-start(bf16[2,9,64,8,64]{2,4,1,3,0:T(8,128)(2,1)} %copy-done.1) | copy-start | bytes 3538948
  174.7 20.8 %all-to-all-start.2 = ((bf16[1,2,64,10,66]{4,1,3,0,2:T(2,128)(2,1)}), bf16[1,2,64,10,66]{4,1,3,0,2:T(2,128)(2,1)S(1)}, u32[]{:S(2)}, u32[]{:S(2)}) async-start(bf16[1,2,64,10,66]{4,1,3,0,2:T(2,128)(2,1)} %copy.255), calls=%async_computation.2 | async-start | bytes 655360 | tf_op jit(solution)/shard_map/all_to_all | solution.py:118
  181.8 277.8 %all-reduce.14.cloned.1.call-start = ((), (), s32[]{:S(2)}) async-start(), calls=%async_computation.6 | async-start | bytes 1703936 | tf_op jit(solution)/shard_map/psum | solution.py:136
  187.2 350.0 %all-gather.8.cloned.1.call-start = ((), (), s32[]{:S(2)}) async-start(), calls=%async_computation.5 | async-start | bytes 2129920 | tf_op jit(solution)/shard_map/all_gather | solution.py:130
  195.7 3.3 copy-start.4
  195.7 3.3 copy-start.11
  199.9 10.5 %all-to-all-start = ((bf16[2,128,128]{2,0,1:T(2,128)(2,1)}), bf16[2,128,128]{2,0,1:T(2,128)(2,1)S(1)}, u32[]{:S(2)}, u32[]{:S(2)}) async-start(bf16[2,128,128]{2,0,1:T(2,128)(2,1)} %copy.240), calls=%async_computation | async-start | bytes 131072 | tf_op jit(solution)/shard_map/all_to_all | solution.py:102
Sparse Core Ops, SparseCore 0:
  10.1 42.7 all-gather.3
  56.2 91.2 all-gather.5
  187.7 271.7 all-reduce.13
  462.6 74.5 all-gather.7
where the time goes:
time: 562 us; the launch traced here: 561 us
  waiting for transfers between devices  424 us (75%)
  local copies, waits for them, and re-layouts  54 us (10%)
  blocking collectives  39.5 us (7%)
  starting transfers between devices  15.2 us (3%)
  between operations  14.4 us (3%)
  other arithmetic  7.87 us (1%)
  matrix products  6.42 us (1%)
    psum x1, waiting for transfers between devices, shards(): conv_total, down_total = lax.psum((conv_part, down_part), ('space', 'chan'))  248 us
    all_gather x1, waiting for transfers between devices, shards(): lax.all_gather(rim_strips(grad_padded), 'space', axis=0, tiled=True)  74.2 us
    all_gather x1, waiting for transfers between devices, shards(): whole_features = lax.all_gather(features, 'chan', axis=1, tiled=True)  44.8 us
    all_gather x1, waiting for transfers between devices, shards(): gathered = lax.all_gather(edge_strips(images), 'space', axis=0, tiled=True)  40.1 us
    all_gather x1, blocking collectives, shards(): lax.all_gather(conv_weight, 'chan', axis=0, tiled=True)  20.6 us
    all_gather x1, blocking collectives, shards(): lax.all_gather(down_weight, 'chan', axis=0, tiled=True)  18.9 us
    all_gather x1, local copies, waits for them, and re-layouts, shards(): gathered = lax.all_gather(edge_strips(images), 'space', axis=0, tiled=True)  11.9 us
  transfers between devices with their start and end apart: 7, of which 6 were waited for; matrix products, arithmetic and copies ran while one was open for 4% of the time, Pallas kernels for 0%

commit v1 on v0

--- a/solution.py
+++ b/solution.py
@@ -127,7 +127,9 @@
     grad_padded = grad_padded.at[:, :, block_rows + 1 : tile_side + 2 : block_rows, :].add(
         stacked[:, :, :, block_rows + 1, :]
     )
-    rim_all = lax.all_gather(rim_strips(grad_padded), "space", axis=0, tiled=True)
+    value = rim_strips(grad_padded)
+    copies = jnp.concatenate([value] * lax.axis_size("space"), axis=0)
+    rim_all = lax.all_to_all(copies, "space", 0, 0, tiled=True)
     returned = bordering(rim_all, partner, orientation)
     features_grad = add_edges(grad_padded[:, :, 1:-1, 1:-1], returned).astype(jnp.bfloat16)
     features_grad = features_grad.reshape(tile_count, chan_part, tile_side * tile_side)

time: 562 us -> 528 us (0.940)
  waiting for transfers between devices: 424 us -> 374 us
  starting transfers between devices: 15.2 us -> 22.4 us
    all_gather x1 -> x0, waiting for transfers between devices: 74.2 us -> none  [shards(): lax.all_gather(rim_strips(grad_padded), 'space', axis=0, tiled=True)]
    psum x1, waiting for transfers between devices: 248 us -> 275 us  [shards(): conv_total, down_total = lax.psum((conv_part, down_part), ('space', 'chan'))]
    all_to_all x0 -> x1, starting transfers between devices: none -> 7.27 us  [shards(): rim_all = lax.all_to_all(copies, 'space', 0, 0, tiled=True)]
    all_to_all x1, waiting for transfers between devices: 7.15 us -> 0.64 us  [shards(): lax.all_to_all(pooled_band, 'chan', split_axis=1, concat_axis=2, tiled=True)]
  transfers between devices with their start and end apart: 7 -> 7, of which waited for: 6 -> 5; matrix products, arithmetic and copies ran while one was open for 4% -> 4% of each run, Pallas kernels for 0% -> 0%
where the time goes in v1:
time: 528 us; the launch traced here: 526 us
  waiting for transfers between devices  374 us (71%)
  local copies, waits for them, and re-layouts  58.5 us (11%)
  blocking collectives  39.9 us (8%)
  starting transfers between devices  22.4 us (4%)
  between operations  14.9 us (3%)
  other arithmetic  10.9 us (2%)
  matrix products  5.72 us (1%)
    psum x1, waiting for transfers between devices, shards(): conv_total, down_total = lax.psum((conv_part, down_part), ('space', 'chan'))  275 us
    all_gather x1, waiting for transfers between devices, shards(): whole_features = lax.all_gather(features, 'chan', axis=1, tiled=True)  44.9 us
    all_gather x1, waiting for transfers between devices, shards(): gathered = lax.all_gather(edge_strips(images), 'space', axis=0, tiled=True)  39.9 us
    all_gather x1, blocking collectives, shards(): lax.all_gather(conv_weight, 'chan', axis=0, tiled=True)  20.6 us
    all_gather x1, blocking collectives, shards(): lax.all_gather(down_weight, 'chan', axis=0, tiled=True)  19.3 us
    all_to_all x1, waiting for transfers between devices, shards(): lax.all_to_all(grad_block[None].astype(jnp.bfloat16), 'chan', split_axis=...  12.7 us
    all_gather x1, local copies, waits for them, and re-layouts, shards(): gathered = lax.all_gather(edge_strips(images), 'space', axis=0, tiled=True)  11.6 us
  transfers between devices with their start and end apart: 7, of which 5 were waited for; matrix products, arithmetic and copies ran while one was open for 4% of the time, Pallas kernels for 0%

profile of v1, /device:TPU:1, one launch (start us, length us, event | category | flops | bytes accessed | tf_op | source)
XLA Modules:
  0.0 526.5 jit_solution(17513769815015657285)
XLA Ops:
  7.2 0.7 all-gather.3.cloned.1.call-update
  8.0 44.9 %all-gather.3.cloned.1.call-done = bf16[2,64,4096]{2,1,0:T(8,128)(2,1)} async-done(((bf16[2,8,4096]{2,1,0:T(8,128)(2,1)}), bf16[2,64,4096]{2,1,0:T(8,128)(2,1)}) %all-gather.3.cloned.1.call-update) | async-done | bytes 1048592 | tf_op jit(solution)/shard_map/all_gather | solution.py:81
  52.8 2.0 copy.217
  55.0 0.9 pad_maximum_fusion
  56.0 0.4 copy.243
  56.4 1.2 reshape.474
  57.6 4.4 all-to-all-start.1
  62.1 20.6 %all_gather.14 = bf16[128,9,64]{2,0,1:T(8,128)(2,1)S(1)} all-gather(bf16[16,9,64]{2,0,1:T(8,128)(2,1)S(1)} %copy-done.6), channel_id=1, replica_groups=mesh['space'=64,'chan'=8] {'chan'}, dimensions={0}, use_global_device_ids=true | all-gather | bytes 165888 | tf_op jit(solution)/shard_map/all_gather | solution.py:89
  82.7 19.3 %all_gather.15 = bf16[128,4,128]{2,1,0:T(4,128)(2,1)S(1)} all-gather(bf16[16,4,128]{2,1,0:T(4,128)(2,1)S(1)} %copy-done.7), channel_id=1, replica_groups=mesh['space'=64,'chan'=8] {'chan'}, dimensions={0}, use_global_device_ids=true | all-gather | bytes 147456 | tf_op jit(solution)/shard_map/all_gather | solution.py:90
  102.2 0.6 fusion.29
  102.8 0.4 reshape.475
  103.2 0.3 copy.244
  103.7 0.2 convolution_bitcast_fusion.2
  104.0 0.5 copy-done.2
  104.4 1.2 copy.246
  105.6 2.6 pad.68
  108.2 39.9 %all-gather.5.cloned.1.call-done = bf16[128,4,64,64]{2,3,0,1:T(8,128)(2,1)} async-done(((bf16[2,4,64,64]{2,3,0,1:T(8,128)(2,1)}), bf16[128,4,64,64]{2,3,0,1:T(8,128)(2,1)}) %all-gather.5.cloned.1.call-update) | async-done | bytes 4194320 | tf_op jit(solution)/shard_map/all_gather | solution.py:84
  148.1 11.6 %copy.224 = bf16[128,4,64,64]{3,2,1,0:T(8,128)(2,1)} copy(bf16[128,4,64,64]{2,3,0,1:T(8,128)(2,1)} %all-gather.5.cloned.1.call-done) | data formatting | bytes 8388608 | tf_op jit(solution)/shard_map/all_gather | solution.py:84
  159.7 4.0 gather_fusion
  164.2 1.5 scatter.14
  165.7 1.4 scatter.15
  167.1 0.2 scatter.16
  167.3 1.4 scatter.19
  169.6 0.2 copy-done.4
  169.9 0.9 multiply_convert_fusion
  170.8 0.3 copy-done.1
  171.1 0.8 convolution_bitcast_fusion
  171.9 0.7 slice_bitcast_fusion.8
  172.6 0.9 fusion.1
  173.5 1.1 copy.255
  174.6 7.1 %all-to-all-start.2 = ((bf16[1,2,64,10,66]{4,1,3,0,2:T(2,128)(2,1)}), bf16[1,2,64,10,66]{4,1,3,0,2:T(2,128)(2,1)S(1)}, u32[]{:S(2)}, u32[]{:S(2)}) async-start(bf16[1,2,64,10,66]{4,1,3,0,2:T(2,128)(2,1)} %copy.255), calls=%async_computation.2 | async-start | bytes 655360 | tf_op jit(solution)/shard_map/all_to_all | solution.py:118
  181.7 0.2 fusion
  181.9 0.8 copy.240
  182.7 12.7 %all-to-all-done.2 = bf16[1,2,64,10,66]{4,1,3,0,2:T(2,128)(2,1)S(1)} async-done(((bf16[1,2,64,10,66]{4,1,3,0,2:T(2,128)(2,1)}), bf16[1,2,64,10,66]{4,1,3,0,2:T(2,128)(2,1)S(1)}, u32[]{:S(2)}, u32[]{:S(2)}) %all-to-all-start.2) | async-done | bytes 168992 | tf_op jit(solution)/shard_map/all_to_all | solution.py:118
  195.4 3.5 all-to-all-start
  199.1 0.9 scatter_fusion
  200.0 0.9 scatter_fusion.1
  200.9 0.2 fusion.28
  201.2 0.2 copy.304
  201.4 0.2 copy.263
  202.7 0.3 copy.264
  202.9 2.3 reshape.476
  205.2 0.6 all-to-all-done
  205.9 7.3 %all-to-all-start.3 = ((f32[64,1,4096]{2,1,0:T(1,128)}), f32[64,1,4096]{2,1,0:T(1,128)S(1)}, u32[]{:S(2)}, u32[]{:S(2)}) async-start(f32[64,1,4096]{2,1,0:T(1,128)} %reshape.476), calls=%async_computation.3 | async-start | bytes 2097152 | tf_op jit(solution)/shard_map/all_to_all | solution.py:132
  213.2 0.5 fusion.15
  213.7 0.8 copy.272
  214.6 3.0 convolution_bitcast_fusion.1
  217.6 0.6 copy.322
  218.3 275.4 %all-reduce.14.cloned.1.call-done = (f32[128,9,64]{2,0,1:T(8,128)}, f32[128,4,128]{2,1,0:T(4,128)}) async-done(((f32[128,9,64]{2,0,1:T(8,128)}, f32[128,4,128]{2,1,0:T(4,128)}), (f32[128,9,64]{2,0,1:T(8,128)}, f32[128,4,128]{2,1,0:T(4,128)})) %all-reduce.14.cloned.1.call-update) | async-done | bytes 557072 | tf_op jit(solution)/shard_map/psum | solution.py:138
  493.7 1.4 dynamic-slice_multiply_fusion.1
  495.1 1.5 dynamic-slice_multiply_fusion
  496.6 0.2 slice.419
  496.8 0.3 copy.302
  497.2 0.5 broadcast.234
  497.7 3.3 reduce.16
  500.9 2.2 reshape.477
  503.1 2.1 gather_fusion.1
  505.6 0.3 copy.266
  505.9 1.8 scatter-add.36
  507.7 0.3 copy.267
  508.1 0.2 slice_add_fusion
  508.3 10.4 %scatter-add.38 = f32[2,8,64,64]{2,1,0,3:T(8,128)S(1)} dynamic-update-slice(f32[2,8,64,64]{2,1,0,3:T(8,128)S(1)} %fusion.23, f32[2,8,1,64]{2,1,0,3:T(8,128)S(1)} %slice_add_fusion, s32[]{:T(128)} %constant.268.clone.1, s32[]{:T(128)} %constant.268.clone.1, s32[]{:T(128)} %constant.280.clone.1, s32[]{:T(128)} %constant.268.clone.1) | dynamic-update-slice | bytes 8196 | tf_op jit(solution)/shard_map/scatter-add | solution.py:42
  518.7 0.3 copy.268
  519.0 0.9 reshape.429
  (138 shorter events, 3.2 us)
Async XLA Ops:
  7.2 45.7 %all-gather.3.cloned.1.call-start = ((), (), s32[]{:S(2)}) async-start(), calls=%async_computation.4 | async-start | bytes 1179648 | tf_op jit(solution)/shard_map/all_gather | solution.py:81
  7.9 48.1 %copy-start.5 = (bf16[2,16,1024]{2,1,0:T(8,128)(2,1)S(1)}, bf16[2,16,1024]{2,1,0:T(8,128)(2,1)}, u32[]{:S(2)}) copy-start(bf16[2,16,1024]{2,1,0:T(8,128)(2,1)} %param.25) | copy-start | bytes 196612
  7.9 54.1 %copy-start.8 = (s32[2,4]{1,0:T(2,128)S(1)}, s32[2,4]{1,0:T(2,128)}, u32[]{:S(2)}) copy-start(s32[2,4]{1,0:T(2,128)} %param.26) | copy-start | bytes 100
  7.9 54.1 %copy-start.6 = (bf16[16,9,64]{2,0,1:T(8,128)(2,1)S(1)}, bf16[16,9,64]{2,0,1:T(8,128)(2,1)}, u32[]{:S(2)}) copy-start(bf16[16,9,64]{2,0,1:T(8,128)(2,1)} %param.23) | copy-start | bytes 55300
  7.9 140.1 %all-gather.5.cloned.1.call-start = ((), (), s32[]{:S(2)}) async-start(), calls=%async_computation.5 | async-start | bytes 8519680 | tf_op jit(solution)/shard_map/all_gather | solution.py:84
  54.9 48.7 %copy-start = (bf16[2,64,4096]{1,2,0:T(8,128)(2,1)}, bf16[2,64,4096]{1,2,0:T(8,128)(2,1)S(1)}, u32[]{:S(2)}) copy-start(bf16[2,64,4096]{1,2,0:T(8,128)(2,1)S(1)} %copy.217) | copy-start | bytes 3145732
  54.9 27.8 %copy-start.9 = (s32[2,4]{1,0:T(2,128)S(1)}, s32[2,4]{1,0:T(2,128)}, u32[]{:S(2)}) copy-start(s32[2,4]{1,0:T(2,128)} %param.27) | copy-start | bytes 100
  54.9 27.8 %copy-start.7 = (bf16[16,4,128]{2,1,0:T(4,128)(2,1)S(1)}, bf16[16,4,128]{2,1,0:T(4,128)(2,1)}, u32[]{:S(2)}) copy-start(bf16[16,4,128]{2,1,0:T(4,128)(2,1)} %param.24) | copy-start | bytes 49156
  57.6 45.2 %all-to-all-start.1 = ((bf16[8,2,2048]{2,1,0:T(2,128)(2,1)}), bf16[8,2,2048]{2,1,0:T(2,128)(2,1)S(1)}, u32[]{:S(2)}, u32[]{:S(2)}) async-start(bf16[8,2,2048]{2,1,0:T(2,128)(2,1)} %reshape.474), calls=%async_computation.1 | async-start | bytes 131072 | tf_op jit(solution)/shard_map/all_to_all | solution.py:103
  103.7 0.7 copy-start.2
  168.8 1.0 copy-start.4
  169.6 1.4 copy-start.1
  171.1 10.6 %copy-start.10 = (bf16[2,128,8,64]{1,3,2,0:T(8,128)(2,1)}, bf16[2,128,8,64]{1,3,2,0:T(8,128)(2,1)S(1)}, u32[]{:S(2)}) copy-start(bf16[2,128,8,64]{1,3,2,0:T(8,128)(2,1)S(1)} %get-tuple-element.122) | copy-start | bytes 786436
  174.6 20.8 %all-to-all-start.2 = ((bf16[1,2,64,10,66]{4,1,3,0,2:T(2,128)(2,1)}), bf16[1,2,64,10,66]{4,1,3,0,2:T(2,128)(2,1)S(1)}, u32[]{:S(2)}, u32[]{:S(2)}) async-start(bf16[1,2,64,10,66]{4,1,3,0,2:T(2,128)(2,1)} %copy.255), calls=%async_computation.2 | async-start | bytes 655360 | tf_op jit(solution)/shard_map/all_to_all | solution.py:118
  195.4 10.5 %all-to-all-start = ((bf16[2,128,128]{2,0,1:T(2,128)(2,1)}), bf16[2,128,128]{2,0,1:T(2,128)(2,1)S(1)}, u32[]{:S(2)}, u32[]{:S(2)}) async-start(bf16[2,128,128]{2,0,1:T(2,128)(2,1)} %copy.240), calls=%async_computation | async-start | bytes 131072 | tf_op jit(solution)/shard_map/all_to_all | solution.py:102
  205.2 8.0 %copy-start.3 = (bf16[2,128,4,32]{3,2,1,0:T(4,128)(2,1)S(1)}, bf16[2,128,4,32]{3,2,1,0:T(4,128)(2,1)}, u32[]{:S(2)}) copy-start(bf16[2,128,4,32]{3,2,1,0:T(4,128)(2,1)} %copy-done.2) | copy-start | bytes 196612
  205.2 8.0 %copy-start.11 = (bf16[2,128,8,64]{1,3,2,0:T(8,128)(2,1)S(1)}, bf16[2,128,8,64]{1,3,2,0:T(8,128)(2,1)}, u32[]{:S(2)}) copy-start(bf16[2,128,8,64]{1,3,2,0:T(8,128)(2,1)} %copy-done.10) | copy-start | bytes 786436
  205.9 291.3 %all-to-all-start.3 = ((f32[64,1,4096]{2,1,0:T(1,128)}), f32[64,1,4096]{2,1,0:T(1,128)S(1)}, u32[]{:S(2)}, u32[]{:S(2)}) async-start(f32[64,1,4096]{2,1,0:T(1,128)} %reshape.476), calls=%async_computation.3 | async-start | bytes 2097152 | tf_op jit(solution)/shard_map/all_to_all | solution.py:132
  213.2 280.6 %all-reduce.14.cloned.1.call-start = ((), (), s32[]{:S(2)}) async-start(), calls=%async_computation.6 | async-start | bytes 1703936 | tf_op jit(solution)/shard_map/psum | solution.py:138
Sparse Core Ops, SparseCore 0:
  10.1 42.7 all-gather.2
  56.8 91.2 all-gather.4
  219.1 274.5 all-reduce.13
